TPU v7x, 32 devices: a whole 2x2x4 slice. The times are simulated.
32 devices in a mesh: rep: 2 (over x), span: 2 (over core), tp: 8 (over z, y).
Axes of the slice: x: 2, y: 2, z: 4, core: 2. Of those that a mesh axis runs over, the one named last changes fastest.
Arguments:
- hidden_in: bfloat16 [16, 128, 6144], P(('rep', 'span'), None, 'tp'), parts along dimension 0, may hold values from -6 to 6
- levels: int32 [16], P(('rep', 'span')), parts along dimension 0, may hold values from 0 to 3
- order: int32 [16], P('rep'), parts along dimension 0, may hold values from 0 to 7, each once
- cache_mask: int32 [16, 8], P('rep'), parts along dimension 0, may hold values 0 or 1
- finished: int32 [2], P('rep'), parts along dimension 0, may hold values from 0 to 7
- cache_kv: bfloat16 [16, 128, 2, 1024], P(('rep', 'span'), None, None, 'tp'), parts along dimension 0, may hold values from -300 to 300
- modulation: bfloat16 [4, 6, 6144], replicated, may hold values from 0.5 to 1.5
- w_qkv: bfloat16 [6144, 3, 1024], P(None, None, 'tp'), may hold values from -0.109375 to 0.109375
- w_out: bfloat16 [1024, 6144], P('tp'), may hold values from -0.375 to 0.375
- w_up: bfloat16 [6144, 4096], P(None, ('span', 'tp')), may hold values from -0.078125 to 0.078125
- w_down: bfloat16 [4096, 6144], P(('span', 'tp')), may hold values from -0.09375 to 0.09375
Outputs:
- layer_out: bfloat16 [16, 128, 6144], P(('rep', 'span'), None, 'tp'), parts along dimension 0
There are 2 independent parts, one for each index of `rep`. A program takes and returns all parts, laid end to end along the dimension named above; an argument that names none is the same for every part. Nothing has to cross between parts.
All inputs are finite; a program needn't handle non-finite values.
Results may differ from a plain program's by a relative error of at most 0.025.
The roundings to bfloat16 on the way count: a program that leaves them out, or rounds other values in their place, can miss the bound.
Values may be sent and summed in bfloat16 or wider, within the bound.
No kernel may reach another device: no remote copies, remote signals or barrier semaphores. Data moves between devices by JAX's collectives and lax.ppermute only.
A program may use at most 128 MiB of HBM per device.

v0:
```python
import math
import jax
import jax.numpy as jnp
from jax import lax
from jax.sharding import PartitionSpec as P

HEAD_DIM = 128
EPSILON = 1e-06
NEGATIVE = -1e30


def normalize(values):
    return values * lax.rsqrt(jnp.mean(values * values, axis=-1, keepdims=True) + EPSILON)


def select_row(source, target):
    matches = jnp.arange(source.shape[0], dtype=jnp.int32) == target
    return jnp.sum(jnp.where(matches.reshape((-1,) + (1,) * (source.ndim - 1)), source, 0), axis=0)


def attend(queries, cache_all, fresh_all, cache_seen, fresh_seen):
    row_count, head_count, head_size = queries.shape
    cache_keys = cache_all[:, :, 0].reshape(-1, head_count, head_size)
    cache_vals = cache_all[:, :, 1].reshape(-1, head_count, head_size)
    fresh_keys = fresh_all[:, :, 0].reshape(-1, head_count, head_size)
    fresh_vals = fresh_all[:, :, 1].reshape(-1, head_count, head_size)
    score_scale = 1.0 / math.sqrt(head_size)
    cache_scores = (
        jnp.einsum("qhd,khd->hqk", queries, cache_keys, preferred_element_type=jnp.float32)
        * score_scale
    )
    fresh_scores = (
        jnp.einsum("qhd,khd->hqk", queries, fresh_keys, preferred_element_type=jnp.float32)
        * score_scale
    )
    cache_scores = jnp.where(cache_seen[None, None, :], cache_scores, NEGATIVE)
    fresh_scores = jnp.where(fresh_seen[None, None, :], fresh_scores, NEGATIVE)
    scores = jnp.concatenate([cache_scores, fresh_scores], axis=2)
    row_max = jnp.max(scores, axis=2, keepdims=True)
    exp_terms = jnp.exp(scores - row_max)
    weights = (exp_terms / jnp.sum(exp_terms, axis=2, keepdims=True)).astype(jnp.bfloat16)
    split_at = cache_keys.shape[0]
    attended = jnp.einsum(
        "hqk,khd->qhd", weights[:, :, :split_at], cache_vals, preferred_element_type=jnp.float32
    )
    attended = attended + jnp.einsum(
        "hqk,khd->qhd", weights[:, :, split_at:], fresh_vals, preferred_element_type=jnp.float32
    )
    return attended.astype(jnp.bfloat16).reshape(row_count, head_count * head_size)


def local(
    hidden_in, levels, order, cache_mask, finished, cache_kv, modulation, w_qkv, w_out, w_up, w_down
):
    span_index = lax.axis_index("span")
    tp_rank = lax.axis_index("tp")
    model_width = modulation.shape[2]
    share_width = hidden_in.shape[2]
    local_count = hidden_in.shape[0]
    row_count = hidden_in.shape[1]
    up_full, down_full = (
        lax.all_gather(w_up, "span", axis=1, tiled=True),
        lax.all_gather(w_down, "span", axis=0, tiled=True),
    )
    mod_table = modulation.reshape(modulation.shape[0], -1)
    picker = (jnp.arange(mod_table.shape[0], dtype=jnp.int32)[None, :] == levels[:, None]).astype(
        jnp.bfloat16
    )
    mod_rows = jnp.dot(picker, mod_table, preferred_element_type=jnp.float32).reshape(
        local_count, 6, model_width
    )
    gathered = lax.all_gather(hidden_in, "tp", axis=2, tiled=True).astype(jnp.float32)
    attn_in = (normalize(gathered) * mod_rows[:, 1][:, None] + mod_rows[:, 0][:, None]).astype(
        jnp.bfloat16
    )
    per_device = w_qkv.shape[2]
    projected = jnp.dot(
        attn_in.reshape(local_count * row_count, model_width),
        w_qkv.reshape(model_width, -1),
        preferred_element_type=jnp.float32,
    )
    projected = projected.astype(jnp.bfloat16).reshape(local_count, row_count, 3, per_device)
    queries = projected[:, :, 0].reshape(local_count, row_count, -1, HEAD_DIM)
    fresh_kv = projected[:, :, 1:]
    cache_all, fresh_all = (
        lax.all_gather(cache_kv, "span", axis=0, tiled=True),
        lax.all_gather(fresh_kv, "span", axis=0, tiled=True),
    )
    positions = jnp.arange(cache_mask.shape[0], dtype=jnp.int32)
    my_spans = span_index * local_count + jnp.arange(local_count, dtype=jnp.int32)
    mask_rows = jax.vmap(lambda target: select_row(cache_mask, target))(my_spans)
    my_order = jax.vmap(lambda target: select_row(order, target))(my_spans)
    cache_seen = jnp.repeat(
        (mask_rows == 1) | (positions[None, :] == finished[0]), row_count, axis=1
    )
    fresh_seen = jnp.repeat(order[None, :] <= my_order[:, None], row_count, axis=1)
    attended = jax.vmap(
        lambda q_rows, c_seen, f_seen: attend(q_rows, cache_all, fresh_all, c_seen, f_seen)
    )(queries, cache_seen, fresh_seen)
    partial_value = jnp.dot(
        attended.reshape(local_count * row_count, -1), w_out, preferred_element_type=jnp.float32
    )
    partial_value = partial_value.reshape(local_count, row_count, model_width)
    mod_share = lax.dynamic_slice_in_dim(mod_rows, tp_rank * share_width, share_width, 2)
    attn_part = lax.psum_scatter(
        partial_value.astype(jnp.bfloat16), "tp", scatter_dimension=2, tiled=True
    ).astype(jnp.float32)
    residual = hidden_in.astype(jnp.float32) + mod_share[:, 2][:, None] * attn_part
    squares = lax.psum(jnp.sum(residual * residual, axis=2), "tp")
    scaled = residual * lax.rsqrt(squares / model_width + EPSILON)[:, :, None]
    mlp_part = (scaled * mod_share[:, 4][:, None] + mod_share[:, 3][:, None]).astype(jnp.bfloat16)
    pre_act = jnp.dot(
        lax.all_gather(mlp_part, "tp", axis=2, tiled=True),
        up_full,
        preferred_element_type=jnp.float32,
    )
    hidden_units = jax.nn.gelu(pre_act).astype(jnp.bfloat16)
    down_terms = jnp.dot(hidden_units, down_full, preferred_element_type=jnp.float32)
    mlp_out = lax.psum_scatter(
        down_terms.astype(jnp.bfloat16), "tp", scatter_dimension=2, tiled=True
    ).astype(jnp.float32)
    result = residual + mod_share[:, 5][:, None] * mlp_out
    return result.astype(jnp.bfloat16)


def solution(mesh):
    placed = (
        P(("rep", "span"), None, "tp"),
        P(("rep", "span")),
        P("rep"),
        P("rep", None),
        P("rep"),
        P(("rep", "span"), None, None, "tp"),
        P(),
        P(None, None, "tp"),
        P("tp", None),
        P(None, ("span", "tp")),
        P(("span", "tp"), None),
    )
    return jax.shard_map(
        local, mesh=mesh, in_specs=placed, out_specs=P(("rep", "span"), None, "tp"), check_vma=False
    )
```

profile of v0, /device:TPU:0, one launch (start us, length us, event | category | flops | bytes accessed | tf_op | source)
XLA Modules:
  0.0 528.1 jit_solution(8121966962387378399)
XLA Ops:
  7.4 0.0 copy-start
  7.4 0.0 all-gather.5.cloned.1.call-start
  7.4 0.7 all-gather.5.cloned.1.call-update
  8.1 0.0 reduce-scatter.3.cloned.1.call-start
  8.1 0.0 copy-start.8
  8.2 0.0 copy-start.10
  8.2 0.0 copy-start.7
  8.2 0.0 copy-start.6
  8.2 0.0 copy-start.9
  8.2 6.8 %copy.29 = bf16[6144,3,128]{0,2,1:T(8,128)(2,1)} copy(bf16[6144,3,128]{2,0,1:T(8,128)(2,1)} %param.18) | data formatting | bytes 9437184 | tf_op args[7]
  15.6 0.1 iota_compare_fusion
  15.7 0.0 copy-done.8
  15.7 0.1 select_reduce_fusion
  15.8 0.1 broadcast_bitcast_fusion.1
  15.9 0.0 copy-done.10
  15.9 0.2 select_reduce_fusion.1
  16.1 0.1 broadcast_compare_fusion
  16.2 0.1 broadcast_bitcast_fusion
  16.3 0.0 copy-done.7
  16.3 2.3 all_gather.19
  18.6 0.0 copy-done.6
  18.6 0.4 fusion.30
  19.0 93.2 %all-gather.5.cloned.1.call-done = bf16[4,128,6144]{2,1,0:T(8,128)(2,1)} async-done(((bf16[4,128,768]{2,1,0:T(8,128)(2,1)}), bf16[4,128,6144]{2,1,0:T(8,128)(2,1)}) %all-gather.5.cloned.1.call-update) | async-done | bytes 6291472 | tf_op jit(solution)/shard_map/all_gather | solution.py:72
  112.2 4.2 fusion
  116.4 0.3 copy-done.2
  116.8 2.7 fusion.3
  119.5 5.8 %convolution_convert_fusion.2 = bf16[512,384]{1,0:T(8,128)(2,1)S(1)} fusion(bf16[512,6144]{1,0:T(8,128)(2,1)S(1)} %bitcast.110, bf16[6144,384]{0,1:T(8,128)(2,1)} %bitcast.111), kind=kOutput, calls=%fused_computation.27 | convolution fusion | flops 2416115712 | bytes 11403264 | tf_op jit(solution)/shard_map/dot_general | solution.py:77
  125.3 0.2 copy.30
  125.5 0.1 reshape.192
  125.6 0.1 slice.60
  125.8 0.2 copy.33
  126.0 2.4 all_gather.20
  128.4 0.1 copy.39
  128.5 0.4 fusion.32
  129.0 0.8 fusion.9
  129.8 0.7 fusion.8
  130.5 0.9 divide_convert_fusion
  131.5 1.3 copy-done.5
  132.8 0.4 fusion.29
  133.2 0.0 copy-done
  133.2 5.4 %convolution_convert_fusion.1 = bf16[4,128,6144]{2,1,0:T(8,128)(2,1)} fusion(bf16[128,6144]{1,0:T(8,128)(2,1)S(1)} %copy-done, f32[128,4,128]{0,2,1:T(8,128)S(1)} %fusion.29, bf16[1024,128,1]{1,0,2:T(8,128)(2,1)S(1)} %bitcast.112, bf16[4,1,128,2048]{3,2,0,1:T(8,128)(2,1)} %copy-done.5), kind=kOutput, calls=%fused_computation.7 | convolution fusion | flops 942800896 | bytes 9437184 | tf_op jit(solution)/shard_map/dot_general | solution.py:100
  138.7 0.0 reduce-scatter.3.cloned.1.call-update
  138.7 0.0 copy-start.3
  138.7 0.0 all-gather.9.cloned.1.call-start
  138.7 0.5 all-gather.9.cloned.1.call-update
  139.3 0.0 all-gather.7.cloned.1.call-start
  139.4 115.7 %reduce-scatter.3.cloned.1.call-done = bf16[4,128,768]{2,1,0:T(8,128)(2,1)} async-done(((bf16[4,128,6144]{2,1,0:T(8,128)(2,1)}), bf16[4,128,768]{2,1,0:T(8,128)(2,1)}) %reduce-scatter.3.cloned.1.call-update) | async-done | bytes 786448 | tf_op jit(solution)/shard_map/reduce_scatter | solution.py:105
  255.1 1.5 multiply_reduce_fusion
  256.6 19.6 %psum.7 = f32[4,128]{1,0:T(4,128)S(1)} all-reduce(f32[4,128]{1,0:T(4,128)S(1)} %multiply_reduce_fusion), channel_id=1, replica_groups=mesh['rep'=2,'span'=2,'tp'=8] {'tp'}, use_global_device_ids=true, to_apply=%region_8.9 | all-reduce | flops 512 | bytes 4096 | tf_op jit(solution)/shard_map/psum | solution.py:109
  276.2 2.4 add_convert_fusion.1
  278.6 0.0 all-gather.7.cloned.1.call-update
  278.6 0.0 all-gather.11.cloned.1.call-start
  278.7 0.5 all-gather.11.cloned.1.call-update
  279.2 0.0 reduce-scatter.5.cloned.1.call-start
  279.3 0.0 all-gather.9.cloned.1.call-done
  279.3 95.3 %all-gather.7.cloned.1.call-done = bf16[4,128,6144]{2,1,0:T(8,128)(2,1)} async-done(((bf16[4,128,768]{2,1,0:T(8,128)(2,1)}), bf16[4,128,6144]{2,1,0:T(8,128)(2,1)}) %all-gather.7.cloned.1.call-update) | async-done | bytes 6291472 | tf_op jit(solution)/shard_map/all_gather | solution.py:113
  374.6 8.2 %fusion.26 = bf16[4,128,512]{2,1,0:T(8,128)(2,1)S(1)} fusion(bf16[4,128,6144]{2,1,0:T(8,128)(2,1)} %all-gather.7.cloned.1.call-done, bf16[6144,512]{1,0:T(8,128)(2,1)} %all-gather.9.cloned.1.call-done), kind=kOutput, calls=%fused_computation.39 | convolution fusion | flops 3223584768 | bytes 13107200 | tf_op jit(solution)/shard_map/dot_general | solution.py:112
  382.8 8.3 %all-gather.11.cloned.1.call-done = bf16[512,6144]{1,0:T(8,128)(2,1)} async-done(((bf16[256,6144]{1,0:T(8,128)(2,1)}), bf16[512,6144]{1,0:T(8,128)(2,1)}) %all-gather.11.cloned.1.call-update) | async-done | bytes 6291472 | tf_op jit(solution)/shard_map/all_gather | solution.py:63
  391.1 8.1 %convolution_convert_fusion = bf16[4,128,6144]{2,1,0:T(8,128)(2,1)} fusion(bf16[4,128,512]{2,1,0:T(8,128)(2,1)S(1)} %fusion.26, bf16[512,6144]{1,0:T(8,128)(2,1)} %all-gather.11.cloned.1.call-done), kind=kOutput, calls=%fused_computation.6 | convolution fusion | flops 3224371200 | bytes 13107200 | tf_op jit(solution)/shard_map/dot_general | solution.py:118
  399.1 0.0 reduce-scatter.5.cloned.1.call-update
  399.2 0.0 copy-start.1
  399.2 118.9 %reduce-scatter.5.cloned.1.call-done = bf16[4,128,768]{2,1,0:T(8,128)(2,1)} async-done(((bf16[4,128,6144]{2,1,0:T(8,128)(2,1)}), bf16[4,128,768]{2,1,0:T(8,128)(2,1)}) %reduce-scatter.5.cloned.1.call-update) | async-done | bytes 786448 | tf_op jit(solution)/shard_map/reduce_scatter | solution.py:119
  518.1 0.0 copy-done.4
  518.1 2.4 add_convert_fusion
  (20 shorter events, 0.3 us)
Async XLA Ops:
  7.4 125.9 %copy-start = (bf16[128,6144]{1,0:T(8,128)(2,1)S(1)}, bf16[128,6144]{1,0:T(8,128)(2,1)}, u32[]{:S(2)}) copy-start(bf16[128,6144]{1,0:T(8,128)(2,1)} %param.19) | copy-start | bytes 4718596
  7.4 104.8 %all-gather.5.cloned.1.call-start = ((), (), s32[]{:S(2)}) async-start(), calls=%async_computation.2 | async-start | bytes 7077888 | tf_op jit(solution)/shard_map/all_gather | solution.py:72
  8.1 247.0 %reduce-scatter.3.cloned.1.call-start = ((), (), s32[]{:S(2)}) async-start(), calls=%async_computation.3 | async-start | bytes 7077888 | tf_op jit(solution)/shard_map/reduce_scatter | solution.py:105
  8.1 7.6 %copy-start.8 = (s32[8,8]{1,0:T(8,128)S(1)}, s32[8,8]{1,0:T(8,128)}, u32[]{:S(2)}) copy-start(s32[8,8]{1,0:T(8,128)} %param.14) | copy-start | bytes 772
  8.2 7.7 %copy-start.10 = (s32[8]{0:T(128)S(1)}, s32[8]{0:T(128)}, u32[]{:S(2)}) copy-start(s32[8]{0:T(128)} %param.13) | copy-start | bytes 100
  8.2 8.1 %copy-start.7 = (bf16[4,128,2,128]{3,2,1,0:T(2,128)(2,1)S(1)}, bf16[4,128,2,128]{3,2,1,0:T(2,128)(2,1)}, u32[]{:S(2)}) copy-start(bf16[4,128,2,128]{3,2,1,0:T(2,128)(2,1)} %param.16) | copy-start | bytes 786436
  8.2 10.4 %copy-start.6 = (bf16[4,6,6144]{2,0,1:T(4,128)(2,1)S(1)}, bf16[4,6,6144]{2,0,1:T(4,128)(2,1)}, u32[]{:S(2)}) copy-start(bf16[4,6,6144]{2,0,1:T(4,128)(2,1)} %param.17) | copy-start | bytes 884740
  8.2 10.4 %copy-start.9 = (s32[4]{0:T(128)S(1)}, s32[4]{0:T(128)}, u32[]{:S(2)}) copy-start(s32[4]{0:T(128)} %param.12) | copy-start | bytes 52
  112.2 4.6 copy-start.2
  131.4 1.3 copy-start.5
  138.7 116.4 %copy-start.3 = (bf16[4,128,768]{2,1,0:T(8,128)(2,1)S(1)}, bf16[4,128,768]{2,1,0:T(8,128)(2,1)}, u32[]{:S(2)}) copy-start(bf16[4,128,768]{2,1,0:T(8,128)(2,1)} %param.11) | copy-start | bytes 2359300
  138.7 140.6 %all-gather.9.cloned.1.call-start = ((), (), s32[]{:S(2)}) async-start(), calls=%async_computation.5 | async-start | bytes 9437184 | tf_op jit(solution)/shard_map/all_gather | solution.py:62
  139.3 235.3 %all-gather.7.cloned.1.call-start = ((), (), s32[]{:S(2)}) async-start(), calls=%async_computation.4 | async-start | bytes 7077888 | tf_op jit(solution)/shard_map/all_gather | solution.py:113
  278.6 112.4 %all-gather.11.cloned.1.call-start = ((), (), s32[]{:S(2)}) async-start(), calls=%async_computation.6 | async-start | bytes 9437184 | tf_op jit(solution)/shard_map/all_gather | solution.py:63
  279.2 238.9 %reduce-scatter.5.cloned.1.call-start = ((), (), s32[]{:S(2)}) async-start(), calls=%async_computation.7 | async-start | bytes 7077888 | tf_op jit(solution)/shard_map/reduce_scatter | solution.py:119
  399.1 119.0 %copy-start.4 = (bf16[4,128,768]{2,1,0:T(8,128)(2,1)S(1)}, bf16[4,128,768]{2,1,0:T(8,128)(2,1)}, u32[]{:S(2)}) copy-start(bf16[4,128,768]{2,1,0:T(8,128)(2,1)} %reduce-scatter.3.cloned.1.call-done) | copy-start | bytes 2359300
  399.2 121.3 %copy-start.1 = (bf16[128,6144]{1,0:T(8,128)(2,1)S(1)}, bf16[128,6144]{1,0:T(8,128)(2,1)}, u32[]{:S(2)}) copy-start(bf16[128,6144]{1,0:T(8,128)(2,1)} %param.19) | copy-start | bytes 4718596
Sparse Core Ops, SparseCore 0:
  10.4 101.7 all-gather.4
  138.8 116.2 reduce-scatter.2
Sparse Core Ops, SparseCore 1:
  140.7 13.8 all-gather.8
  278.7 95.8 all-gather.6
  376.0 15.0 all-gather.10
  399.2 118.8 reduce-scatter.4
where the time goes:
time: 529 us; the launch traced here: 528 us
  waiting for transfers between devices  433 us (82%)
  matrix products  29.6 us (6%)
  blocking collectives  24.2 us (5%)
  between operations  16 us (3%)
  other arithmetic  15.4 us (3%)
  local copies, waits for them, and re-layouts  9.57 us (2%)
    reduce_scatter x1, waiting for transfers between devices, local(): lax.psum_scatter(down_terms.astype(jnp.bfloat16), 'tp', scatter_dimension...  119 us
    reduce_scatter x1, waiting for transfers between devices, local(): lax.psum_scatter(partial_value.astype(jnp.bfloat16), 'tp', scatter_dimens...  116 us
    all_gather x1, waiting for transfers between devices, local(): lax.all_gather(mlp_part, 'tp', axis=2, tiled=True)  95.3 us
    all_gather x1, waiting for transfers between devices, local(): lax.all_gather(hidden_in, 'tp', axis=2, tiled=True).astype(jnp.float32)  93.2 us
    psum x1, blocking collectives, local(): squares = lax.psum(jnp.sum(residual * residual, axis=2), 'tp')  19.6 us
  transfers between devices with their start and end apart: 6, of which 5 were waited for; matrix products, arithmetic and copies ran while one was open for 4% of the time, Pallas kernels for 0%

commit v1 on v0

--- a/solution.py
+++ b/solution.py
@@ -7,6 +7,12 @@
 HEAD_DIM = 128
 EPSILON = 1e-06
 NEGATIVE = -1e30
+
+
+def produce_groups(inp, out_dim):
+    met_up = list(inp.shape[1:])
+    met_up[out_dim] *= inp.shape[0]
+    return jnp.moveaxis(inp, 0, out_dim).reshape(met_up)
 
 
 def normalize(values):
@@ -52,6 +58,30 @@
 def local(
     hidden_in, levels, order, cache_mask, finished, cache_kv, modulation, w_qkv, w_out, w_up, w_down
 ):
+
+    def answer_the_groups(point, a_name, on_dim):
+        devs = jax.lax.axis_size(a_name)
+        pieces_in = [(c, (c + 1) % devs) for c in range(devs)]
+        by_place = [(to_i, s) for s, to_i in pieces_in]
+        b_now, z1 = ([], [])
+        for rr in range(devs - 1):
+            if rr % 2 == 0:
+                next_value = jax.lax.ppermute(
+                    b_now[-1] if b_now else point, axis_name=a_name, perm=pieces_in
+                )
+                b_now.append(next_value)
+            else:
+                all_values = jax.lax.ppermute(
+                    z1[-1] if z1 else point, axis_name=a_name, perm=by_place
+                )
+                z1.append(all_values)
+        plain = jnp.stack([*b_now[::-1], point, *z1], axis=0)
+        t_next = jax.lax.axis_index(a_name)
+        z_new = len(b_now)
+        current_block = t_next - z_new
+        plain = plain[(jnp.arange(devs) - current_block) % devs]
+        return produce_groups(plain, on_dim)
+
     span_index = lax.axis_index("span")
     tp_rank = lax.axis_index("tp")
     model_width = modulation.shape[2]
@@ -69,7 +99,7 @@
     mod_rows = jnp.dot(picker, mod_table, preferred_element_type=jnp.float32).reshape(
         local_count, 6, model_width
     )
-    gathered = lax.all_gather(hidden_in, "tp", axis=2, tiled=True).astype(jnp.float32)
+    gathered = answer_the_groups(hidden_in, "tp", 2).astype(jnp.float32)
     attn_in = (normalize(gathered) * mod_rows[:, 1][:, None] + mod_rows[:, 0][:, None]).astype(
         jnp.bfloat16
     )

time: 529 us -> 605 us (1.14)
  local copies, waits for them, and re-layouts: 9.57 us -> 53.7 us
  starting transfers between devices: 0.21 us -> 15.6 us
  other arithmetic: 15.4 us -> 29.3 us
    all_gather x1 -> x0, waiting for transfers between devices: 93.2 us -> none  [local(): lax.all_gather(hidden_in, 'tp', axis=2, tiled=True).astype(jnp.float32)]
    ppermute x0 -> x7, waiting for transfers between devices: none -> 92.2 us  [the longest x4 67.7 us: answer_the_groups(): jax.lax.ppermute(b_now[-1] if b_now else point, axis_name=a_name, perm=pi...]
    convert_element_type x0 -> x2, local copies, waits for them, and re-layouts: none -> 21.3 us  [the longest x1 12.6 us: local(): gathered = answer_the_groups(hidden_in, 'tp', 2).astype(jnp.float32)]
    ppermute x0 -> x7, starting transfers between devices: none -> 15.4 us  [the longest x4 7.93 us: answer_the_groups(): jax.lax.ppermute(b_now[-1] if b_now else point, axis_name=a_name, perm=pi...]
    unnamed x29 -> x44, local copies, waits for them, and re-layouts: 8.82 us -> 19.9 us
    convert_element_type x0 -> x1, other arithmetic: none -> 8.98 us  [local(): gathered = answer_the_groups(hidden_in, 'tp', 2).astype(jnp.float32)]
    convert_element_type x1, other arithmetic: 2.7 us -> 9.85 us  [local(): (normalize(gathered) * mod_rows[:, 1][:, None] + mod_rows[:, 0][:, None])...]
    gather x0 -> x1, local copies, waits for them, and re-layouts: none -> 6.37 us  [answer_the_groups(): plain = plain[(jnp.arange(devs) - current_block) % devs]]
  transfers between devices with their start and end apart: 6 -> 12, of which waited for: 5 -> 9; matrix products, arithmetic and copies ran while one was open for 4% -> 6% of each run, Pallas kernels for 0% -> 0%
where the time goes in v1:
time: 605 us; the launch traced here: 604 us
  waiting for transfers between devices  433 us (72%)
  local copies, waits for them, and re-layouts  53.7 us (9%)
  matrix products  32.3 us (5%)
  other arithmetic  29.3 us (5%)
  blocking collectives  24.2 us (4%)
  between operations  15.9 us (3%)
  starting transfers between devices  15.6 us (3%)
    reduce_scatter x1, waiting for transfers between devices, local(): lax.psum_scatter(down_terms.astype(jnp.bfloat16), 'tp', scatter_dimension...  119 us
    reduce_scatter x1, waiting for transfers between devices, local(): lax.psum_scatter(partial_value.astype(jnp.bfloat16), 'tp', scatter_dimens...  116 us
    all_gather x1, waiting for transfers between devices, local(): lax.all_gather(mlp_part, 'tp', axis=2, tiled=True)  95.3 us
    ppermute x4, waiting for transfers between devices, answer_the_groups(): jax.lax.ppermute(b_now[-1] if b_now else point, axis_name=a_name, perm=pi...  67.7 us
    ppermute x3, waiting for transfers between devices, answer_the_groups(): jax.lax.ppermute(z1[-1] if z1 else point, axis_name=a_name, perm=by_place)  24.5 us
    unnamed x44, local copies, waits for them, and re-layouts  19.9 us
    psum x1, blocking collectives, local(): squares = lax.psum(jnp.sum(residual * residual, axis=2), 'tp')  19.6 us
    convert_element_type x1, local copies, waits for them, and re-layouts, local(): gathered = answer_the_groups(hidden_in, 'tp', 2).astype(jnp.float32)  12.6 us
  transfers between devices with their start and end apart: 12, of which 9 were waited for; matrix products, arithmetic and copies ran while one was open for 6% of the time, Pallas kernels for 0%

profile of v1, /device:TPU:0, one launch (start us, length us, event | category | flops | bytes accessed | tf_op | source)
XLA Modules:
  0.0 603.6 jit_solution(10436621663848118650)
XLA Ops:
  7.4 3.0 collective-permute-start
  10.3 3.1 collective-permute-start.4
  14.1 0.1 iota_compare_fusion
  14.2 0.8 select_reduce_fusion
  14.9 1.3 fusion.30
  16.3 28.0 %collective-permute-done = bf16[4,128,768]{2,1,0:T(8,128)(2,1)S(1)} collective-permute-done((bf16[4,128,768]{2,1,0:T(8,128)(2,1)}, bf16[4,128,768]{2,1,0:T(8,128)(2,1)S(1)}, u32[]{:S(2)}, u32[]{:S(2)}) %collective-permute-start) | collective-permute-done | bytes 786464 | tf_op jit(solution)/shard_map/ppermute | solution.py:69
  44.3 2.4 collective-permute-start.1
  46.7 0.7 slice_bitcast_fusion.6
  47.3 19.0 %collective-permute-done.1 = bf16[4,128,768]{2,1,0:T(8,128)(2,1)S(1)} collective-permute-done((bf16[4,128,768]{2,1,0:T(8,128)(2,1)S(1)}, bf16[4,128,768]{2,1,0:T(8,128)(2,1)S(1)}, u32[]{:S(2)}, u32[]{:S(2)}) %collective-permute-start.1) | collective-permute-done | bytes 786464 | tf_op jit(solution)/shard_map/ppermute | solution.py:69
  66.4 7.0 %copy.41 = bf16[6144,3,128]{0,2,1:T(8,128)(2,1)} copy(bf16[6144,3,128]{2,0,1:T(8,128)(2,1)} %param.18) | data formatting | bytes 9437184 | tf_op args[7]
  73.4 0.1 broadcast_bitcast_fusion.1
  73.5 0.2 select_reduce_fusion.1
  73.7 0.1 broadcast_compare_fusion
  73.8 4.4 collective-permute-start.5
  78.2 20.6 %collective-permute-done.2 = bf16[4,128,768]{2,1,0:T(8,128)(2,1)} collective-permute-done((bf16[4,128,768]{2,1,0:T(8,128)(2,1)S(1)}, bf16[4,128,768]{2,1,0:T(8,128)(2,1)}, u32[]{:S(2)}, u32[]{:S(2)}) %collective-permute-start.2) | collective-permute-done | bytes 786464 | tf_op jit(solution)/shard_map/ppermute | solution.py:69
  98.8 2.6 collective-permute-start.3
  101.4 0.1 broadcast_bitcast_fusion
  101.6 2.3 all_gather.15
  103.9 0.7 fusion.41
  104.6 16.0 %collective-permute-done.5 = bf16[4,128,768]{2,1,0:T(8,128)(2,1)} collective-permute-done((bf16[4,128,768]{2,1,0:T(8,128)(2,1)}, bf16[4,128,768]{2,1,0:T(8,128)(2,1)}, u32[]{:S(2)}, u32[]{:S(2)}) %collective-permute-start.5) | collective-permute-done | bytes 786464 | tf_op jit(solution)/shard_map/ppermute | solution.py:74
  120.7 2.1 bitcast_dynamic-update-slice_fusion.7
  122.7 2.1 bitcast_dynamic-update-slice_fusion.6
  124.8 0.9 bitcast_dynamic-update-slice_fusion.5
  125.8 0.9 bitcast_dynamic-update-slice_fusion.4
  126.7 1.0 bitcast_dynamic-update-slice_fusion.3
  127.7 2.1 bitcast_dynamic-update-slice_fusion.2
  129.7 2.1 bitcast_dynamic-update-slice_fusion.1
  131.8 8.5 %collective-permute-done.6 = bf16[4,128,768]{2,1,0:T(8,128)(2,1)S(1)} collective-permute-done((bf16[4,128,768]{2,1,0:T(8,128)(2,1)}, bf16[4,128,768]{2,1,0:T(8,128)(2,1)S(1)}, u32[]{:S(2)}, u32[]{:S(2)}) %collective-permute-start.6) | collective-permute-done | bytes 786464 | tf_op jit(solution)/shard_map/ppermute | solution.py:74
  140.3 0.9 bitcast_dynamic-update-slice_fusion
  141.3 6.4 %gather_fusion = bf16[8,4,128,768]{3,2,1,0:T(8,128)(2,1)} fusion(bf16[8,4,128,768]{3,2,1,0:T(8,128)(2,1)} %bitcast_dynamic-update-slice_fusion, s32[1024]{0:T(1024)S(1)} %pad_clamp_fusion), kind=kCustom, calls=%fused_computation | custom fusion | bytes 12582944 | tf_op jit(solution)/shard_map/gather | solution.py:82
  147.7 9.0 %convert_bitcast_fusion = f32[4,128,8,768]{3,1,0,2:T(8,128)} fusion(bf16[8,4,128,768]{3,2,1,0:T(8,128)(2,1)} %gather_fusion), kind=kLoop, calls=%fused_computation.2 | loop fusion | flops 3145728 | bytes 18874368 | tf_op jit(solution)/shard_map/convert_element_type | solution.py:102
  156.6 1.3 fusion
  158.0 12.6 %copy.39 = f32[4,128,8,768]{1,3,2,0:T(8,128)} copy(f32[4,128,8,768]{3,1,0,2:T(8,128)} %convert_bitcast_fusion) | data formatting | bytes 25165824 | tf_op jit(solution)/shard_map/convert_element_type | solution.py:102
  170.6 9.8 %fusion.3 = bf16[4,128,6144]{1,2,0:T(8,128)(2,1)} fusion(f32[4,128,8,768]{1,3,2,0:T(8,128)} %copy.39, f32[4,6144]{1,0:T(4,128)S(1)} %copy-done.11, f32[4,6144]{1,0:T(4,128)S(1)} %get-tuple-element.13, f32[4,128]{1,0:T(4,128)S(1)} %add_rsqrt_fusion.1), kind=kLoop, calls=%fused_computation.7 | loop fusion | flops 12582912 | bytes 19073024 | tf_op jit(solution)/shard_map/convert_element_type | solution.py:103
  180.4 8.7 %copy.40 = bf16[4,128,6144]{2,1,0:T(8,128)(2,1)} copy(bf16[4,128,6144]{1,2,0:T(8,128)(2,1)} %fusion.3) | data formatting | bytes 12582912 | tf_op jit(solution)/shard_map/convert_element_type | solution.py:103
  189.1 7.6 %convolution_convert_fusion.2 = bf16[512,384]{1,0:T(8,128)(2,1)S(1)} fusion(bf16[512,6144]{1,0:T(8,128)(2,1)} %bitcast.138, bf16[6144,384]{0,1:T(8,128)(2,1)} %bitcast.139), kind=kOutput, calls=%fused_computation.29 | convolution fusion | flops 2416115712 | bytes 11403264 | tf_op jit(solution)/shard_map/dot_general | solution.py:107
  196.7 0.2 copy.42
  196.9 0.1 reshape.286
  197.0 0.8 slice.62
  197.9 1.1 copy.45
  199.0 2.4 all_gather.16
  201.4 0.7 fusion.42
  202.1 0.1 copy.51
  202.3 0.4 fusion.32
  202.7 0.8 fusion.9
  203.6 0.7 fusion.8
  204.3 0.9 divide_convert_fusion
  205.2 1.3 copy-done.4
  206.5 0.4 fusion.29
  207.0 5.4 convolution_convert_fusion.1
  212.4 0.0 all-gather.6.cloned.1.call-start
  212.5 0.5 all-gather.6.cloned.1.call-update
  213.1 0.8 dynamic-slice_bitcast_fusion.2
  213.9 116.4 %reduce-scatter.3.cloned.1.call-done = bf16[4,128,768]{2,1,0:T(8,128)(2,1)} async-done(((bf16[4,128,6144]{2,1,0:T(8,128)(2,1)}), bf16[4,128,768]{2,1,0:T(8,128)(2,1)}) %reduce-scatter.3.cloned.1.call-update) | async-done | bytes 786448 | tf_op jit(solution)/shard_map/reduce_scatter | solution.py:135
  330.2 1.5 multiply_reduce_fusion
  331.7 19.6 %psum.7 = f32[4,128]{1,0:T(4,128)S(1)} all-reduce(f32[4,128]{1,0:T(4,128)S(1)} %multiply_reduce_fusion), channel_id=1, replica_groups=mesh['rep'=2,'span'=2,'tp'=8] {'tp'}, use_global_device_ids=true, to_apply=%region_8.9 | all-reduce | flops 512 | bytes 4096 | tf_op jit(solution)/shard_map/psum | solution.py:139
  351.3 2.4 add_convert_fusion.1
  353.8 0.5 all-gather.8.cloned.1.call-update
  354.4 95.3 %all-gather.4.cloned.1.call-done = bf16[4,128,6144]{2,1,0:T(8,128)(2,1)} async-done(((bf16[4,128,768]{2,1,0:T(8,128)(2,1)}), bf16[4,128,6144]{2,1,0:T(8,128)(2,1)}) %all-gather.4.cloned.1.call-update) | async-done | bytes 6291472 | tf_op jit(solution)/shard_map/all_gather | solution.py:143
  449.7 8.2 %fusion.26 = bf16[4,128,512]{2,1,0:T(8,128)(2,1)S(1)} fusion(bf16[4,128,6144]{2,1,0:T(8,128)(2,1)} %all-gather.4.cloned.1.call-done, bf16[6144,512]{1,0:T(8,128)(2,1)} %all-gather.6.cloned.1.call-done), kind=kOutput, calls=%fused_computation.41 | convolution fusion | flops 3223584768 | bytes 13107200 | tf_op jit(solution)/shard_map/dot_general | solution.py:142
  457.9 8.3 %all-gather.8.cloned.1.call-done = bf16[512,6144]{1,0:T(8,128)(2,1)} async-done(((bf16[256,6144]{1,0:T(8,128)(2,1)}), bf16[512,6144]{1,0:T(8,128)(2,1)}) %all-gather.8.cloned.1.call-update) | async-done | bytes 6291472 | tf_op jit(solution)/shard_map/all_gather | solution.py:93
  466.2 8.1 %convolution_convert_fusion = bf16[4,128,6144]{2,1,0:T(8,128)(2,1)} fusion(bf16[4,128,512]{2,1,0:T(8,128)(2,1)S(1)} %fusion.26, bf16[512,6144]{1,0:T(8,128)(2,1)} %all-gather.8.cloned.1.call-done), kind=kOutput, calls=%fused_computation.8 | convolution fusion | flops 3224371200 | bytes 13107200 | tf_op jit(solution)/shard_map/dot_general | solution.py:148
  474.3 119.3 %reduce-scatter.5.cloned.1.call-done = bf16[4,128,768]{2,1,0:T(8,128)(2,1)} async-done(((bf16[4,128,6144]{2,1,0:T(8,128)(2,1)}), bf16[4,128,768]{2,1,0:T(8,128)(2,1)}) %reduce-scatter.5.cloned.1.call-update) | async-done | bytes 786448 | tf_op jit(solution)/shard_map/reduce_scatter | solution.py:149
  593.6 2.4 add_convert_fusion
  (53 shorter events, 0.4 us)
Async XLA Ops:
  7.4 199.6 %copy-start = (bf16[128,6144]{1,0:T(8,128)(2,1)S(1)}, bf16[128,6144]{1,0:T(8,128)(2,1)}, u32[]{:S(2)}) copy-start(bf16[128,6144]{1,0:T(8,128)(2,1)} %param.19) | copy-start | bytes 4718596
  7.4 322.8 %reduce-scatter.3.cloned.1.call-start = ((), (), s32[]{:S(2)}) async-start(), calls=%async_computation.2 | async-start | bytes 7077888 | tf_op jit(solution)/shard_map/reduce_scatter | solution.py:135
  7.4 36.9 %collective-permute-start = (bf16[4,128,768]{2,1,0:T(8,128)(2,1)}, bf16[4,128,768]{2,1,0:T(8,128)(2,1)S(1)}, u32[]{:S(2)}, u32[]{:S(2)}) collective-permute-start(bf16[4,128,768]{2,1,0:T(8,128)(2,1)} %param.11), channel_id=1, source_target_pairs={{0,1},{1,2},{2,3},{3,4},{4,5},{5,6},{6,7},{7,0},{8,9},{9,10},{10,1... | collective-permute-start | bytes 2359304 | tf_op jit(solution)/shard_map/ppermute | solution.py:69
  10.3 63.4 %collective-permute-start.4 = (bf16[4,128,768]{2,1,0:T(8,128)(2,1)}, bf16[4,128,768]{2,1,0:T(8,128)(2,1)}, u32[]{:S(2)}, u32[]{:S(2)}) collective-permute-start(bf16[4,128,768]{2,1,0:T(8,128)(2,1)} %param.11), channel_id=1, source_target_pairs={{1,0},{2,1},{3,2},{4,3},{5,4},{6,5},{7,6},{0,7},{9,8},{10,9},{11,1... | collective-permute-start | bytes 2359304 | tf_op jit(solution)/shard_map/ppermute | solution.py:74
  16.3 30.4 %copy-start.5 = (f32[4,6,6144]{2,0,1:T(4,128)}, f32[4,6,6144]{2,0,1:T(4,128)S(1)}, u32[]{:S(2)}) copy-start(f32[4,6,6144]{2,0,1:T(4,128)S(1)} %fusion.30) | copy-start | bytes 1769476
  44.3 22.1 %copy-start.7 = (bf16[4,128,768]{2,1,0:T(8,128)(2,1)}, bf16[4,128,768]{2,1,0:T(8,128)(2,1)S(1)}, u32[]{:S(2)}) copy-start(bf16[4,128,768]{2,1,0:T(8,128)(2,1)S(1)} %collective-permute-done) | copy-start | bytes 2359300
  44.3 22.1 %collective-permute-start.1 = (bf16[4,128,768]{2,1,0:T(8,128)(2,1)S(1)}, bf16[4,128,768]{2,1,0:T(8,128)(2,1)S(1)}, u32[]{:S(2)}, u32[]{:S(2)}) collective-permute-start(bf16[4,128,768]{2,1,0:T(8,128)(2,1)S(1)} %collective-permute-done), channel_id=1, source_target_pairs={{0,1},{1,2},{2,3},{3,4},{4,5},{5,6},{6,7},{7,0},{8,9},{9,10},{10,1... | collective-permute-start | bytes 2359304 | tf_op jit(solution)/shard_map/ppermute | solution.py:69
  66.4 7.0 %copy-start.9 = (bf16[4,128,768]{2,1,0:T(8,128)(2,1)}, bf16[4,128,768]{2,1,0:T(8,128)(2,1)S(1)}, u32[]{:S(2)}) copy-start(bf16[4,128,768]{2,1,0:T(8,128)(2,1)S(1)} %collective-permute-done.1) | copy-start | bytes 2359300
  66.4 32.4 %collective-permute-start.2 = (bf16[4,128,768]{2,1,0:T(8,128)(2,1)S(1)}, bf16[4,128,768]{2,1,0:T(8,128)(2,1)}, u32[]{:S(2)}, u32[]{:S(2)}) collective-permute-start(bf16[4,128,768]{2,1,0:T(8,128)(2,1)S(1)} %collective-permute-done.1), channel_id=1, source_target_pairs={{0,1},{1,2},{2,3},{3,4},{4,5},{5,6},{6,7},{7,0},{8,9},{9,10},{10,1... | collective-permute-start | bytes 2359304 | tf_op jit(solution)/shard_map/ppermute | solution.py:69
  66.4 7.1 %copy-start.14 = (s32[8]{0:T(128)S(1)}, s32[8]{0:T(128)}, u32[]{:S(2)}) copy-start(s32[8]{0:T(128)} %param.13) | copy-start | bytes 100
  66.4 35.1 %copy-start.12 = (bf16[4,128,2,128]{3,2,1,0:T(2,128)(2,1)S(1)}, bf16[4,128,2,128]{3,2,1,0:T(2,128)(2,1)}, u32[]{:S(2)}) copy-start(bf16[4,128,2,128]{3,2,1,0:T(2,128)(2,1)} %param.16) | copy-start | bytes 786436
  73.4 53.3 %copy-start.2 = (bf16[4,128,768]{2,1,0:T(8,128)(2,1)S(1)}, bf16[4,128,768]{2,1,0:T(8,128)(2,1)}, u32[]{:S(2)}) copy-start(bf16[4,128,768]{2,1,0:T(8,128)(2,1)} %param.11) | copy-start | bytes 2359300
  73.8 46.9 %collective-permute-start.5 = (bf16[4,128,768]{2,1,0:T(8,128)(2,1)}, bf16[4,128,768]{2,1,0:T(8,128)(2,1)}, u32[]{:S(2)}, u32[]{:S(2)}) collective-permute-start(bf16[4,128,768]{2,1,0:T(8,128)(2,1)} %collective-permute-done.4), channel_id=1, source_target_pairs={{1,0},{2,1},{3,2},{4,3},{5,4},{6,5},{7,6},{0,7},{9,8},{10,9},{11,1... | collective-permute-start | bytes 2359304 | tf_op jit(solution)/shard_map/ppermute | solution.py:74
  98.8 21.9 %collective-permute-start.3 = (bf16[4,128,768]{2,1,0:T(8,128)(2,1)}, bf16[4,128,768]{2,1,0:T(8,128)(2,1)}, u32[]{:S(2)}, u32[]{:S(2)}) collective-permute-start(bf16[4,128,768]{2,1,0:T(8,128)(2,1)} %collective-permute-done.2), channel_id=1, source_target_pairs={{0,1},{1,2},{2,3},{3,4},{4,5},{5,6},{6,7},{7,0},{8,9},{9,10},{10,1... | collective-permute-start | bytes 2359304 | tf_op jit(solution)/shard_map/ppermute | solution.py:69
  101.5 23.3 %copy-start.10 = (bf16[4,128,768]{2,1,0:T(8,128)(2,1)S(1)}, bf16[4,128,768]{2,1,0:T(8,128)(2,1)}, u32[]{:S(2)}) copy-start(bf16[4,128,768]{2,1,0:T(8,128)(2,1)} %copy-done.9) | copy-start | bytes 2359300
  101.6 24.2 %copy-start.8 = (bf16[4,128,768]{2,1,0:T(8,128)(2,1)S(1)}, bf16[4,128,768]{2,1,0:T(8,128)(2,1)}, u32[]{:S(2)}) copy-start(bf16[4,128,768]{2,1,0:T(8,128)(2,1)} %copy-done.7) | copy-start | bytes 2359300
  120.7 19.7 %collective-permute-start.6 = (bf16[4,128,768]{2,1,0:T(8,128)(2,1)}, bf16[4,128,768]{2,1,0:T(8,128)(2,1)S(1)}, u32[]{:S(2)}, u32[]{:S(2)}) collective-permute-start(bf16[4,128,768]{2,1,0:T(8,128)(2,1)} %collective-permute-done.5), channel_id=1, source_target_pairs={{1,0},{2,1},{3,2},{4,3},{5,4},{6,5},{7,6},{0,7},{9,8},{10,9},{11,1... | collective-permute-start | bytes 2359304 | tf_op jit(solution)/shard_map/ppermute | solution.py:74
  147.7 9.0 %copy-start.1 = (bf16[8,4,128,768]{3,2,1,0:T(8,128)(2,1)S(1)}, bf16[8,4,128,768]{3,2,1,0:T(8,128)(2,1)}, u32[]{:S(2)}) copy-start(bf16[8,4,128,768]{3,2,1,0:T(8,128)(2,1)} %gather_fusion) | copy-start | bytes 18874372
  157.9 12.6 %copy-start.11 = (f32[4,6144]{1,0:T(4,128)S(1)}, f32[4,6144]{1,0:T(4,128)}, u32[]{:S(2)}) copy-start(f32[4,6144]{1,0:T(4,128)} %get-tuple-element.14) | copy-start | bytes 294916
  197.0 5.7 copy-start.6
  203.5 3.0 copy-start.13
  205.2 1.3 copy-start.4
  212.4 142.0 %all-gather.6.cloned.1.call-start = ((), (), s32[]{:S(2)}) async-start(), calls=%async_computation.4 | async-start | bytes 9437184 | tf_op jit(solution)/shard_map/all_gather | solution.py:92
  213.0 236.7 %all-gather.4.cloned.1.call-start = ((), (), s32[]{:S(2)}) async-start(), calls=%async_computation.3 | async-start | bytes 7077888 | tf_op jit(solution)/shard_map/all_gather | solution.py:143
  353.8 112.4 %all-gather.8.cloned.1.call-start = ((), (), s32[]{:S(2)}) async-start(), calls=%async_computation.5 | async-start | bytes 9437184 | tf_op jit(solution)/shard_map/all_gather | solution.py:93
  354.4 239.2 %reduce-scatter.5.cloned.1.call-start = ((), (), s32[]{:S(2)}) async-start(), calls=%async_computation.6 | async-start | bytes 7077888 | tf_op jit(solution)/shard_map/reduce_scatter | solution.py:149
  474.3 119.3 %copy-start.3 = (bf16[4,128,768]{2,1,0:T(8,128)(2,1)S(1)}, bf16[4,128,768]{2,1,0:T(8,128)(2,1)}, u32[]{:S(2)}) copy-start(bf16[4,128,768]{2,1,0:T(8,128)(2,1)} %reduce-scatter.3.cloned.1.call-done) | copy-start | bytes 2359300
Sparse Core Ops, SparseCore 0:
  212.6 117.5 reduce-scatter.2
  474.4 119.1 reduce-scatter.4
Sparse Core Ops, SparseCore 1:
  214.5 15.2 all-gather.5
  353.9 95.8 all-gather.3
  451.1 15.0 all-gather.7
